TPU v7x, 256 devices: a whole 4x4x8 slice. The times are simulated.
256 devices in a mesh: gz: 32 (over x, z), gx: 8 (over y, core).
Axes of the slice: x: 4, y: 4, z: 8, core: 2. Of those that a mesh axis runs over, the one named last changes fastest.
Arguments:
- u_field: bfloat16 [2, 512, 2048, 128], P(None, 'gx', 'gz'), may hold values from -64 to 64, as said below
- w_field: bfloat16 [2, 512, 2048, 128], P(None, 'gx', 'gz'), may hold values from -64 to 64, as said below
Outputs:
- modes: float32 [2, 512, 2048, 128], P(None, 'gx', 'gz')
- factor_r: float32 [2, 128, 128], replicated
Inputs may be any that keep to these rules, and one draw needn't show every extreme that they name: `u_field`: velocity values of a snapshot. `w_field`: velocity values of a snapshot.
All inputs are finite; a program needn't handle non-finite values.
Results may differ from a plain program's by a relative error of at most 0.0003.
Values may be sent and summed in bfloat16 or wider, within the bound.
No kernel may reach another device: no remote copies, remote signals or barrier semaphores. Data moves between devices by JAX's collectives and lax.ppermute only.
A program may use at most 64 MiB of HBM per device.

v0:
```python
import jax
import jax.numpy as jnp
from jax import lax
from jax.sharding import PartitionSpec as P

span_step = 0.75


def with_halo(cells, sides, width):
    for axis, dim in sides:
        count = lax.axis_size(axis)
        head = lax.slice_in_dim(cells, 0, width, axis=dim)
        tail = lax.slice_in_dim(cells, cells.shape[dim] - width, cells.shape[dim], axis=dim)
        cells = jnp.concatenate(
            [
                lax.ppermute(tail, axis, [(i, (i + 1) % count) for i in range(count)]),
                cells,
                lax.ppermute(head, axis, [((i + 1) % count, i) for i in range(count)]),
            ],
            axis=dim,
        )
    return cells


def local(u_field, w_field):
    planes, rows_x, rows_z, snaps = u_field.shape
    padded_u = with_halo(u_field, (("gz", 2),), 2).astype(jnp.float32)
    padded_w = with_halo(w_field, (("gx", 1),), 2).astype(jnp.float32)
    span_diff = 8.0 * (padded_u[:, :, 3:-1] - padded_u[:, :, 1:-3]) - (
        padded_u[:, :, 4:] - padded_u[:, :, :-4]
    )
    stream_diff = 8.0 * (padded_w[:, 3:-1] - padded_w[:, 1:-3]) - (
        padded_w[:, 4:] - padded_w[:, :-4]
    )
    vorticity = span_diff / (12.0 * span_step) - stream_diff / 12.0
    columns = vorticity.reshape(planes, rows_x * rows_z, snaps)
    gram_local = jnp.einsum(
        "pcs,pct->pst",
        columns,
        columns,
        precision=lax.Precision.HIGHEST,
        preferred_element_type=jnp.float32,
    )
    gram_sum = lax.psum(gram_local, ("gz", "gx"))
    total_cells = rows_x * rows_z * lax.axis_size("gz") * lax.axis_size("gx")
    gram = gram_sum / total_cells
    lower = jnp.linalg.cholesky(gram)
    identity_matrix = jnp.broadcast_to(jnp.eye(snaps, dtype=gram.dtype), lower.shape)
    lower_inverse = lax.linalg.triangular_solve(lower, identity_matrix, left_side=True, lower=True)
    inverse_r = jnp.transpose(lower_inverse, (0, 2, 1))
    modes = jnp.einsum(
        "pcs,pst->pct",
        columns,
        inverse_r,
        precision=lax.Precision.HIGHEST,
        preferred_element_type=jnp.float32,
    )
    modes = modes.reshape(planes, rows_x, rows_z, snaps)
    factor_r = jnp.transpose(lower, (0, 2, 1))
    return (modes, factor_r)


def solution(mesh):
    return jax.shard_map(
        local,
        mesh=mesh,
        in_specs=(P(None, "gx", "gz", None), P(None, "gx", "gz", None)),
        out_specs=(P(None, "gx", "gz", None), P()),
        check_vma=False,
    )
```

profile of v0, /device:TPU:2, one launch (start us, length us, event | category | flops | bytes accessed | tf_op | source)
XLA Modules:
  0.0 339.1 jit_solution(9191449530525586369)
XLA Ops:
  7.2 0.0 copy-start.1
  7.2 0.0 all-reduce.2.cloned.1.call-start
  7.2 1.3 fusion.13
  8.5 2.0 collective-permute-start
  10.5 4.0 %collective-permute-start.1 = (bf16[2,64,2,128]{3,2,1,0:T(2,128)(2,1)S(1)}, bf16[2,64,2,128]{3,2,1,0:T(2,128)(2,1)S(1)}, u32[]{:S(2)}, u32[]{:S(2)}) collective-permute-start(bf16[2,64,2,128]{3,2,1,0:T(2,128)(2,1)S(1)} %get-tuple-element.7), channel_id=1, source_target_pairs={{8,0},{16,8},{24,16},{32,24},{40,32},{48,40},{56,48},{64,56},{72,6... | collective-permute-start | bytes 196616 | tf_op jit(solution)/shard_map/ppermute | solution.py:18
  14.5 0.9 fusion.14
  15.4 0.0 collective-permute-start.2
  15.4 2.9 collective-permute-start.3
  18.4 0.0 collective-permute-done
  18.4 0.0 collective-permute-done.1
  18.4 2.8 maximum_convert_fusion
  21.2 0.0 collective-permute-done.2
  21.2 0.0 collective-permute-done.3
  21.2 0.0 copy-done.1
  21.2 0.3 maximum_convert_fusion.1
  21.6 2.8 fusion.2
  24.4 0.0 copy-start
  24.4 1.9 copy-done
  26.3 7.5 %fusion.15 = f32[2,128,128]{1,2,0:T(8,128)} fusion(f32[2,4096,128]{2,1,0:T(8,128)S(1)} %bitcast.17), kind=kOutput, calls=%fused_computation.29 | convolution fusion | flops 1610612736 | bytes 4325376 | tf_op jit(solution)/shard_map/pcs,pct->pst/dot_general | solution.py:37
  33.8 0.0 all-reduce.2.cloned.1.call-update
  33.9 245.2 %all-reduce.2.cloned.1.call-done = f32[2,128,128]{1,2,0:T(8,128)} async-done(((f32[2,128,128]{1,2,0:T(8,128)}), f32[2,128,128]{1,2,0:T(8,128)}) %all-reduce.2.cloned.1.call-update) | async-done | bytes 131088 | tf_op jit(solution)/shard_map/psum | solution.py:44
  279.1 0.9 broadcast_multiply_fusion
  280.0 0.1 copy.10
  280.1 0.9 fusion.9
  281.0 23.6 %custom-call.7 = f32[2,128,128]{2,1,0:T(8,128)S(1)} custom-call(f32[2,128,128]{2,1,0:T(8,128)S(1)} %fusion.9), custom_call_target="Cholesky" | custom-call | tf_op jit(solution)/shard_map/jit(cholesky)/cholesky | solution.py:47
  304.7 0.1 compare_reduce_fusion
  304.8 0.1 fusion.10
  304.9 19.7 %custom-call.8 = f32[2,1,128,128]{2,3,1,0:T(8,128)S(1)} custom-call(f32[2,1,128,128]{3,2,1,0:T(8,128)S(1)} %get-tuple-element.11), custom_call_target="InvertDiagBlocksLowerTriangular" | custom-call | tf_op jit(solution)/shard_map/triangular_solve | solution.py:49
  324.6 0.4 fusion.7
  325.0 6.5 %fusion.16 = f32[2,4096,128]{2,1,0:T(8,128)} fusion(f32[2,4096,128]{2,1,0:T(8,128)} %bitcast.18, f32[2,128,128]{2,1,0:T(8,128)S(1)} %fusion.7), kind=kOutput, calls=%fused_computation.30 | convolution fusion | flops 1610612736 | bytes 8519680 | tf_op jit(solution)/shard_map/pcs,pst->pct/dot_general | solution.py:51
  331.5 0.8 copy.11
  (4 shorter events, 0.1 us)
Async XLA Ops:
  7.2 14.1 %copy-start.1 = (bf16[2,64,64,128]{3,2,1,0:T(8,128)(2,1)S(1)}, bf16[2,64,64,128]{3,2,1,0:T(8,128)(2,1)}, u32[]{:S(2)}) copy-start(bf16[2,64,64,128]{3,2,1,0:T(8,128)(2,1)} %param.3) | copy-start | bytes 6291460
  7.2 271.9 %all-reduce.2.cloned.1.call-start = ((), (), s32[]{:S(2)}) async-start(), calls=%async_computation | async-start | bytes 262144 | tf_op jit(solution)/shard_map/psum | solution.py:44
  8.5 9.9 %collective-permute-start = (bf16[2,64,2,128]{3,2,1,0:T(2,128)(2,1)S(1)}, bf16[2,64,2,128]{3,2,1,0:T(2,128)(2,1)S(1)}, u32[]{:S(2)}, u32[]{:S(2)}) collective-permute-start(bf16[2,64,2,128]{3,2,1,0:T(2,128)(2,1)S(1)} %get-tuple-element.6), channel_id=1, source_target_pairs={{0,8},{8,16},{16,24},{24,32},{32,40},{40,48},{48,56},{56,64},{64,7... | collective-permute-start | bytes 196616 | tf_op jit(solution)/shard_map/ppermute | solution.py:16
  10.5 7.9 %collective-permute-start.1 = (bf16[2,64,2,128]{3,2,1,0:T(2,128)(2,1)S(1)}, bf16[2,64,2,128]{3,2,1,0:T(2,128)(2,1)S(1)}, u32[]{:S(2)}, u32[]{:S(2)}) collective-permute-start(bf16[2,64,2,128]{3,2,1,0:T(2,128)(2,1)S(1)} %get-tuple-element.7), channel_id=1, source_target_pairs={{8,0},{16,8},{24,16},{32,24},{40,32},{48,40},{56,48},{64,56},{72,6... | collective-permute-start | bytes 196616 | tf_op jit(solution)/shard_map/ppermute | solution.py:18
  15.4 5.8 %collective-permute-start.2 = (bf16[2,2,64,128]{3,2,1,0:T(8,128)(2,1)S(1)}, bf16[2,2,64,128]{3,2,1,0:T(8,128)(2,1)S(1)}, u32[]{:S(2)}, u32[]{:S(2)}) collective-permute-start(bf16[2,2,64,128]{3,2,1,0:T(8,128)(2,1)S(1)} %get-tuple-element.8), channel_id=1, source_target_pairs={{0,1},{1,2},{2,3},{3,4},{4,5},{5,6},{6,7},{7,0},{8,9},{9,10},{10,1... | collective-permute-start | bytes 196616 | tf_op jit(solution)/shard_map/ppermute | solution.py:16
  15.4 5.8 %collective-permute-start.3 = (bf16[2,2,64,128]{3,2,1,0:T(8,128)(2,1)S(1)}, bf16[2,2,64,128]{3,2,1,0:T(8,128)(2,1)S(1)}, u32[]{:S(2)}, u32[]{:S(2)}) collective-permute-start(bf16[2,2,64,128]{3,2,1,0:T(8,128)(2,1)S(1)} %get-tuple-element.9), channel_id=1, source_target_pairs={{1,0},{2,1},{3,2},{4,3},{5,4},{6,5},{7,6},{0,7},{9,8},{10,9},{11,1... | collective-permute-start | bytes 196616 | tf_op jit(solution)/shard_map/ppermute | solution.py:18
  24.4 1.9 copy-start
Sparse Core Ops, SparseCore 0:
  34.0 245.0 all-reduce.1
where the time goes:
time: 339 us
  waiting for transfers between devices  245 us (72%)
  other arithmetic  51.3 us (15%)
  matrix products  14.5 us (4%)
  between operations  14.2 us (4%)
  starting transfers between devices  8.99 us (3%)
  local copies, waits for them, and re-layouts  4.96 us (1%)
    psum x1, waiting for transfers between devices, local(): gram_sum = lax.psum(gram_local, ('gz', 'gx'))  245 us
    another operation x4, other arithmetic, local(): lower = jnp.linalg.cholesky(gram)  23.8 us
    another operation x2, other arithmetic, local(): lax.linalg.triangular_solve(lower, identity_matrix, left_side=True, lower...  19.7 us
    dot_general x1, matrix products, local(): jnp.einsum('pcs,pct->pst', columns, columns, precision=lax.Precision.HIGH...  7.54 us
    ppermute x2, starting transfers between devices, with_halo(): lax.ppermute(head, axis, [((i + 1) % count, i) for i in range(count)])  6.94 us
  transfers between devices with their start and end apart: 5, of which 1 were waited for; matrix products, arithmetic and copies ran while one was open for 1% of the time, Pallas kernels for 0%

commit v1 on v0

--- a/solution.py
+++ b/solution.py
@@ -41,7 +41,7 @@
         precision=lax.Precision.HIGHEST,
         preferred_element_type=jnp.float32,
     )
-    gram_sum = lax.psum(gram_local, ("gz", "gx"))
+    gram_sum = jnp.sum(lax.all_gather(gram_local, ("gz", "gx")), axis=0)
     total_cells = rows_x * rows_z * lax.axis_size("gz") * lax.axis_size("gx")
     gram = gram_sum / total_cells
     lower = jnp.linalg.cholesky(gram)

time: 339 us -> 257 us (0.76)
  waiting for transfers between devices: 245 us -> 151 us
  other arithmetic: 51.3 us -> 61.8 us
    psum x1 -> x0, waiting for transfers between devices: 245 us -> none  [local(): gram_sum = lax.psum(gram_local, ('gz', 'gx'))]
    all_gather x0 -> x1, waiting for transfers between devices: none -> 151 us  [local(): gram_sum = jnp.sum(lax.all_gather(gram_local, ('gz', 'gx')), axis=0)]
    reduce_sum x0 -> x1, other arithmetic: none -> 12.2 us  [local(): gram_sum = jnp.sum(lax.all_gather(gram_local, ('gz', 'gx')), axis=0)]
where the time goes in v1:
time: 257 us; the launch traced here: 255 us
  waiting for transfers between devices  151 us (59%)
  other arithmetic  61.8 us (24%)
  matrix products  14.5 us (6%)
  between operations  14.2 us (6%)
  starting transfers between devices  8.99 us (3%)
  local copies, waits for them, and re-layouts  5.06 us (2%)
    all_gather x1, waiting for transfers between devices, local(): gram_sum = jnp.sum(lax.all_gather(gram_local, ('gz', 'gx')), axis=0)  151 us
    another operation x4, other arithmetic, local(): lower = jnp.linalg.cholesky(gram)  23.8 us
    another operation x2, other arithmetic, local(): lax.linalg.triangular_solve(lower, identity_matrix, left_side=True, lower...  19.7 us
    reduce_sum x1, other arithmetic, local(): gram_sum = jnp.sum(lax.all_gather(gram_local, ('gz', 'gx')), axis=0)  12.2 us
    dot_general x1, matrix products, local(): jnp.einsum('pcs,pct->pst', columns, columns, precision=lax.Precision.HIGH...  7.62 us
    ppermute x2, starting transfers between devices, with_halo(): lax.ppermute(head, axis, [((i + 1) % count, i) for i in range(count)])  6.94 us
    dot_general x1, matrix products, local(): jnp.einsum('pcs,pst->pct', columns, inverse_r, precision=lax.Precision.HI...  6.55 us
  transfers between devices with their start and end apart: 5, of which 1 were waited for; matrix products, arithmetic and copies ran while one was open for 1% of the time, Pallas kernels for 0%

profile of v1, /device:TPU:2, one launch (start us, length us, event | category | flops | bytes accessed | tf_op | source)
XLA Modules:
  0.0 255.4 jit_solution(11881680217798394827)
XLA Ops:
  7.2 0.0 copy-start.1
  7.2 0.0 all-gather.3.cloned.1.call-start
  7.2 1.3 fusion.13
  8.5 2.0 collective-permute-start
  10.5 4.0 %collective-permute-start.1 = (bf16[2,64,2,128]{3,2,1,0:T(2,128)(2,1)S(1)}, bf16[2,64,2,128]{3,2,1,0:T(2,128)(2,1)S(1)}, u32[]{:S(2)}, u32[]{:S(2)}) collective-permute-start(bf16[2,64,2,128]{3,2,1,0:T(2,128)(2,1)S(1)} %get-tuple-element.9), channel_id=1, source_target_pairs={{8,0},{16,8},{24,16},{32,24},{40,32},{48,40},{56,48},{64,56},{72,6... | collective-permute-start | bytes 196616 | tf_op jit(solution)/shard_map/ppermute | solution.py:18
  14.5 0.9 fusion.14
  15.4 0.0 collective-permute-start.2
  15.4 2.9 %collective-permute-start.3 = (bf16[2,2,64,128]{3,2,1,0:T(8,128)(2,1)S(1)}, bf16[2,2,64,128]{3,2,1,0:T(8,128)(2,1)S(1)}, u32[]{:S(2)}, u32[]{:S(2)}) collective-permute-start(bf16[2,2,64,128]{3,2,1,0:T(8,128)(2,1)S(1)} %get-tuple-element.11), channel_id=1, source_target_pairs={{1,0},{2,1},{3,2},{4,3},{5,4},{6,5},{7,6},{0,7},{9,8},{10,9},{11,1... | collective-permute-start | bytes 196616 | tf_op jit(solution)/shard_map/ppermute | solution.py:18
  18.4 0.0 collective-permute-done
  18.4 0.0 collective-permute-done.1
  18.4 2.8 %maximum_convert_fusion = f32[2,64,68,128]{3,2,1,0:T(8,128)S(1)} fusion(bf16[2,64,2,128]{3,2,1,0:T(2,128)(2,1)S(1)} %collective-permute-done.1, bf16[2,64,64,128]{3,2,1,0:T(8,128)(2,1)} %param.2, bf16[2,64,2,128]{3,2,1,0:T(2,128)(2,1)S(1)} %collective-permute-done), kind=kLoop, calls=%fused_computation.11 | loop fusion | flops 6684672 | bytes 6684672 | tf_op jit(solution)/shard_map/convert_element_type | solution.py:27
  21.1 0.0 collective-permute-done.2
  21.2 0.0 collective-permute-done.3
  21.2 0.0 copy-done.1
  21.2 0.3 maximum_convert_fusion.1
  21.5 2.8 %fusion.2 = f32[2,64,64,128]{3,2,1,0:T(8,128)S(1)} fusion(f32[2,68,64,128]{3,2,1,0:T(8,128)S(1)} %maximum_convert_fusion.1, f32[2,64,68,128]{3,2,1,0:T(8,128)S(1)} %maximum_convert_fusion), kind=kLoop, calls=%fused_computation.3 | loop fusion | flops 11534336 | bytes 37748736 | tf_op jit(solution)/shard_map/sub | solution.py:35
  24.3 0.0 copy-start
  24.3 2.0 copy-done
  26.3 7.6 %fusion.15 = f32[2,128,128]{2,1,0:T(8,128)} fusion(f32[2,4096,128]{2,1,0:T(8,128)S(1)} %bitcast.18), kind=kOutput, calls=%fused_computation.28 | convolution fusion | flops 1610612736 | bytes 4325376 | tf_op jit(solution)/shard_map/pcs,pct->pst/dot_general | solution.py:37
  34.0 0.0 all-gather.3.cloned.1.call-update
  34.0 150.8 %all-gather.3.cloned.1.call-done = f32[512,128,128]{2,1,0:T(8,128)} async-done(((f32[2,128,128]{2,1,0:T(8,128)}), f32[512,128,128]{2,1,0:T(8,128)}) %all-gather.3.cloned.1.call-update) | async-done | bytes 33554448 | tf_op jit(solution)/shard_map/all_gather | solution.py:44
  184.9 12.2 %reduce_sum.11 = f32[2,128,128]{2,1,0:T(8,128)S(1)} reduce(f32[256,2,128,128]{3,2,1,0:T(8,128)} %bitcast.20, f32[]{:T(128)} %constant.51.clone.1), dimensions={0}, to_apply=%region_0.0 | reduce | flops 8355840 | bytes 33685508 | tf_op jit(solution)/shard_map/reduce_sum | solution.py:44
  197.1 0.1 copy.11
  197.2 23.6 %custom-call.7 = f32[2,128,128]{2,1,0:T(8,128)S(1)} custom-call(f32[2,128,128]{2,1,0:T(8,128)S(1)} %fusion.9), custom_call_target="Cholesky" | custom-call | tf_op jit(solution)/shard_map/jit(cholesky)/cholesky | solution.py:47
  220.9 0.1 compare_reduce_fusion
  221.0 0.1 fusion.10
  221.1 19.7 %custom-call.8 = f32[2,1,128,128]{2,3,1,0:T(8,128)S(1)} custom-call(f32[2,1,128,128]{3,2,1,0:T(8,128)S(1)} %get-tuple-element.13), custom_call_target="InvertDiagBlocksLowerTriangular" | custom-call | tf_op jit(solution)/shard_map/triangular_solve | solution.py:49
  240.8 0.4 fusion.7
  241.2 6.5 %fusion.16 = f32[2,4096,128]{2,1,0:T(8,128)} fusion(f32[2,4096,128]{2,1,0:T(8,128)} %bitcast.19, f32[2,128,128]{2,1,0:T(8,128)S(1)} %fusion.7), kind=kOutput, calls=%fused_computation.29 | convolution fusion | flops 1610612736 | bytes 8519680 | tf_op jit(solution)/shard_map/pcs,pst->pct/dot_general | solution.py:51
  247.8 0.8 copy.13
  (5 shorter events, 0.1 us)
Async XLA Ops:
  7.2 14.0 %copy-start.1 = (bf16[2,64,64,128]{3,2,1,0:T(8,128)(2,1)S(1)}, bf16[2,64,64,128]{3,2,1,0:T(8,128)(2,1)}, u32[]{:S(2)}) copy-start(bf16[2,64,64,128]{3,2,1,0:T(8,128)(2,1)} %param.3) | copy-start | bytes 6291460
  7.2 177.7 %all-gather.3.cloned.1.call-start = ((), (), s32[]{:S(2)}) async-start(), calls=%async_computation | async-start | bytes 33685504 | tf_op jit(solution)/shard_map/all_gather | solution.py:44
  8.5 9.9 %collective-permute-start = (bf16[2,64,2,128]{3,2,1,0:T(2,128)(2,1)S(1)}, bf16[2,64,2,128]{3,2,1,0:T(2,128)(2,1)S(1)}, u32[]{:S(2)}, u32[]{:S(2)}) collective-permute-start(bf16[2,64,2,128]{3,2,1,0:T(2,128)(2,1)S(1)} %get-tuple-element.8), channel_id=1, source_target_pairs={{0,8},{8,16},{16,24},{24,32},{32,40},{40,48},{48,56},{56,64},{64,7... | collective-permute-start | bytes 196616 | tf_op jit(solution)/shard_map/ppermute | solution.py:16
  10.5 7.9 %collective-permute-start.1 = (bf16[2,64,2,128]{3,2,1,0:T(2,128)(2,1)S(1)}, bf16[2,64,2,128]{3,2,1,0:T(2,128)(2,1)S(1)}, u32[]{:S(2)}, u32[]{:S(2)}) collective-permute-start(bf16[2,64,2,128]{3,2,1,0:T(2,128)(2,1)S(1)} %get-tuple-element.9), channel_id=1, source_target_pairs={{8,0},{16,8},{24,16},{32,24},{40,32},{48,40},{56,48},{64,56},{72,6... | collective-permute-start | bytes 196616 | tf_op jit(solution)/shard_map/ppermute | solution.py:18
  15.4 5.8 %collective-permute-start.2 = (bf16[2,2,64,128]{3,2,1,0:T(8,128)(2,1)S(1)}, bf16[2,2,64,128]{3,2,1,0:T(8,128)(2,1)S(1)}, u32[]{:S(2)}, u32[]{:S(2)}) collective-permute-start(bf16[2,2,64,128]{3,2,1,0:T(8,128)(2,1)S(1)} %get-tuple-element.10), channel_id=1, source_target_pairs={{0,1},{1,2},{2,3},{3,4},{4,5},{5,6},{6,7},{7,0},{8,9},{9,10},{10,1... | collective-permute-start | bytes 196616 | tf_op jit(solution)/shard_map/ppermute | solution.py:16
  15.4 5.7 %collective-permute-start.3 = (bf16[2,2,64,128]{3,2,1,0:T(8,128)(2,1)S(1)}, bf16[2,2,64,128]{3,2,1,0:T(8,128)(2,1)S(1)}, u32[]{:S(2)}, u32[]{:S(2)}) collective-permute-start(bf16[2,2,64,128]{3,2,1,0:T(8,128)(2,1)S(1)} %get-tuple-element.11), channel_id=1, source_target_pairs={{1,0},{2,1},{3,2},{4,3},{5,4},{6,5},{7,6},{0,7},{9,8},{10,9},{11,1... | collective-permute-start | bytes 196616 | tf_op jit(solution)/shard_map/ppermute | solution.py:18
  24.3 2.0 copy-start
Sparse Core Ops, SparseCore 0:
  34.1 150.7 all-gather.2
